TPU v7x, 512 devices: a whole 4x4x16 slice. The times are simulated.
512 devices in a mesh: dp: 32 (over z_lo, x), fly: 16 (over z_hi, y, core).
Axes of the slice: x: 4, y: 4, z: 16 (z_hi: 2, z_lo: 8; z = z_hi * 8 + z_lo), core: 2. Of those that a mesh axis runs over, the one named last changes fastest.
Arguments:
- tokens: bfloat16 [4096, 8192], P('dp', 'fly'), may hold values from -6 to 6
- hidden_grad: bfloat16 [4096, 16384], P('dp', 'fly'), may hold values from -6 to 6
- w_up: bfloat16 [6, 256, 16384], P(None, 'dp', 'fly'), may hold values from -0.15625 to 0.15625
- pattern: int32 [6, 64], P(None, 'fly'), may hold values 0 or 1
Outputs:
- input_grad: bfloat16 [4096, 8192], P('dp', 'fly')
- weight_grad: float32 [6, 256, 16384], P(None, 'dp', 'fly')
Inputs may be any that keep to these rules, and one draw needn't show every extreme that they name: pattern[t, f] is 1 where block f of factor t is kept and 0 where it is dropped.
All inputs are finite; a program needn't handle non-finite values.
Results may differ from a plain program's by a relative error of at most 0.0049.
Values may be sent and summed in bfloat16 or wider, within the bound.
No kernel may reach another device: no remote copies, remote signals or barrier semaphores. Data moves between devices by JAX's collectives and lax.ppermute only.
A program may use at most 64 MiB of HBM per device.

v0:
```python
import jax
import jax.numpy as jnp
from jax import lax
from jax.sharding import PartitionSpec as P

BS = 256


def partner_2(block, axis, bit):
    count = lax.axis_size(axis)
    route = []
    for low in range(count):
        high = low | 1 << bit
        if high != low and high < count:
            route += [(low, high), (high, low)]
    return lax.ppermute(block, axis, route)


def shifted(value, axis, by):
    devices = lax.axis_size(axis)
    return lax.ppermute(value, axis, [(i, (i + by) % devices) for i in range(devices)])


def flip_blocks(values, stride):
    if stride == 0:
        return values
    row_count, block_count, inner_size = values.shape
    shaped = values.reshape(row_count, block_count // (2 * stride), 2, stride, inner_size)
    return shaped[:, :, ::-1].reshape(row_count, block_count, inner_size)


def stride_of(factor):
    return 0 if factor == 0 else 2 ** (factor - 1)


def pick_rows(stacked, index, replicas):
    return lax.dynamic_index_in_dim(stacked, index % replicas, 1, keepdims=False)


def body(tokens, hidden_grad, w_up, pattern):
    row_count, local_width = tokens.shape
    factor_count = w_up.shape[0]
    hidden_width = hidden_grad.shape[1]
    local_blocks = local_width // BS
    group_width = hidden_width // local_blocks
    weights = lax.all_gather(w_up, "dp", axis=1, tiled=True)
    keep_cols = jnp.broadcast_to(pattern[:, :, None], (factor_count, pattern.shape[1], BS)).reshape(
        factor_count, hidden_width
    )
    masked = (weights * keep_cols.astype(jnp.bfloat16)[:, None, :]).reshape(
        factor_count, BS, local_blocks, group_width
    )
    keep_f = keep_cols.astype(jnp.float32)
    token_blocks = tokens.reshape(row_count, local_blocks, BS)
    gathered = []
    for factor in range(factor_count):
        stride = stride_of(factor)
        if stride < local_blocks:
            gathered.append(flip_blocks(token_blocks, stride))
        else:
            bit_number = (stride // local_blocks).bit_length() - 1
            partner = partner_2(tokens, "fly", bit_number)
            gathered.append(partner.reshape(row_count, local_blocks, BS))
    pre_act = jnp.zeros((row_count, local_blocks, group_width), jnp.float32)
    for factor in range(factor_count):
        pre_act = pre_act + jnp.einsum(
            "ngb,bgc->ngc", gathered[factor], masked[factor], preferred_element_type=jnp.float32
        )
    squash = jax.nn.sigmoid(pre_act)
    derivative = squash * (1.0 + pre_act * (1.0 - squash))
    grad_pre = (
        hidden_grad.reshape(row_count, local_blocks, group_width).astype(jnp.float32) * derivative
    ).astype(jnp.bfloat16)
    input_total = jnp.zeros((row_count, local_blocks, BS), jnp.float32)
    for factor in range(factor_count):
        stride = stride_of(factor)
        contrib = jnp.einsum(
            "ngc,bgc->ngb", grad_pre, masked[factor], preferred_element_type=jnp.float32
        )
        if stride < local_blocks:
            input_total = input_total + flip_blocks(contrib, stride)
        else:
            bit_number = (stride // local_blocks).bit_length() - 1
            returned = partner_2(contrib.reshape(row_count, local_width), "fly", bit_number)
            input_total = input_total + returned.reshape(row_count, local_blocks, BS)
    input_grad = input_total.reshape(row_count, local_width).astype(jnp.bfloat16)
    replicas = lax.axis_size("dp")
    place = lax.axis_index("dp")
    row_share = BS // replicas
    terms = []
    for factor in range(factor_count):
        product_term = jnp.einsum(
            "ngb,ngc->bgc", gathered[factor], grad_pre, preferred_element_type=jnp.float32
        )
        terms.append(product_term.reshape(BS, hidden_width) * keep_f[factor][None, :])
    term_stack = jnp.stack(terms).reshape(factor_count, replicas, row_share, hidden_width)

    def turn_one(step, carry):
        return shifted(carry, "dp", 1) + pick_rows(
            term_stack, place - step - 2 + 2 * replicas, replicas
        )

    summed = lax.fori_loop(
        0, replicas - 1, turn_one, pick_rows(term_stack, place - 1 + replicas, replicas)
    )
    weight_grad = summed * (1.0 / replicas)
    return (input_grad, weight_grad)


def solution(mesh):
    return jax.shard_map(
        body,
        mesh=mesh,
        in_specs=(P("dp", "fly"), P("dp", "fly"), P(None, "dp", "fly"), P(None, "fly")),
        out_specs=(P("dp", "fly"), P(None, "dp", "fly")),
        check_vma=False,
    )
```

profile of v0, /device:TPU:8, one launch (start us, length us, event | category | flops | bytes accessed | tf_op | source)
XLA Modules:
  0.0 881.5 jit_solution(7239345191191575717)
XLA Ops:
  9.6 15.7 %collective-permute-start.4 = (bf16[128,512]{0,1:T(8,128)(2,1)}, bf16[128,512]{0,1:T(8,128)(2,1)}, u32[]{:S(2)}, u32[]{:S(2)}) collective-permute-start(bf16[128,512]{0,1:T(8,128)(2,1)} %copy.43), channel_id=1, source_target_pairs={{0,8},{8,0},{1,9},{9,1},{2,10},{10,2},{3,11},{11,3},{4,12},{12,4},... | collective-permute-start | bytes 393224 | tf_op jit(solution)/shard_map/ppermute | solution.py:16
  25.3 4.2 collective-permute-start.3
  29.5 3.3 collective-permute-start.2
  40.2 209.0 %all-gather.2.cloned.1.call-done = bf16[6,256,1024]{2,1,0:T(8,128)(2,1)} async-done(((bf16[6,8,1024]{2,1,0:T(8,128)(2,1)}), bf16[6,256,1024]{2,1,0:T(8,128)(2,1)}) %all-gather.2.cloned.1.call-update) | async-done | bytes 3145744 | tf_op jit(solution)/shard_map/all_gather | solution.py:46
  276.4 5.6 collective-permute-start.8
  282.1 6.0 collective-permute-start.7
  288.1 3.3 collective-permute-start.6
  293.5 2.3 copy.67
  295.7 3.1 reshape.263
  298.8 2.3 copy.68
  301.1 3.1 reshape.264
  306.5 3.1 reshape.265
  311.8 3.1 reshape.266
  316.2 3.2 reshape.267
  320.7 3.2 reshape.268
  326.3 2.6 copy-done.9
  328.9 542.7 %while.17 = (s32[]{:T(128)}, f32[6,8,1024]{2,1,0:T(8,128)S(1)}, s32[]{:T(128)}, f32[6,32,8,1024]{3,2,1,0:T(8,128)}, s32[]{:T(128)}, /*index=5*/s32[]{:T(128)}, s32[]{:T(128)}, s32[]{:T(128)}, s32[]{:T(128)}) while((s32[]{:T(128)}, f32[6,8,1024]{2,1,0:T(8,128)S(1)}, s32[]{:T(128)}, f32[6,32,8,1024]{3,2,1,0:T(8,128)}, s32[]{:T(128)}, ...), condition=%wide.region_1.2_spmd, body=%wide.region_0.1_spmd.sunk | while | flops 49170 | bytes 1376560 | solution.py:103
  330.8 16.0 %collective-permute-done = f32[6,8,1024]{2,1,0:T(8,128)S(1)} collective-permute-done((f32[6,8,1024]{2,1,0:T(8,128)S(1)}, f32[6,8,1024]{2,1,0:T(8,128)S(1)}, u32[]{:S(2)}, u32[]{:S(2)}) %collective-permute-start) | collective-permute-done | bytes 196640 | tf_op jit(solution)/shard_map/while/body/eval_jaxpr/ppermute | solution.py:21
  349.7 15.1 %collective-permute-done = f32[6,8,1024]{2,1,0:T(8,128)S(1)} collective-permute-done((f32[6,8,1024]{2,1,0:T(8,128)S(1)}, f32[6,8,1024]{2,1,0:T(8,128)S(1)}, u32[]{:S(2)}, u32[]{:S(2)}) %collective-permute-start) | collective-permute-done | bytes 196640 | tf_op jit(solution)/shard_map/while/body/eval_jaxpr/ppermute | solution.py:21
  367.7 14.3 %collective-permute-done = f32[6,8,1024]{2,1,0:T(8,128)S(1)} collective-permute-done((f32[6,8,1024]{2,1,0:T(8,128)S(1)}, f32[6,8,1024]{2,1,0:T(8,128)S(1)}, u32[]{:S(2)}, u32[]{:S(2)}) %collective-permute-start) | collective-permute-done | bytes 196640 | tf_op jit(solution)/shard_map/while/body/eval_jaxpr/ppermute | solution.py:21
  385.0 14.3 %collective-permute-done = f32[6,8,1024]{2,1,0:T(8,128)S(1)} collective-permute-done((f32[6,8,1024]{2,1,0:T(8,128)S(1)}, f32[6,8,1024]{2,1,0:T(8,128)S(1)}, u32[]{:S(2)}, u32[]{:S(2)}) %collective-permute-start) | collective-permute-done | bytes 196640 | tf_op jit(solution)/shard_map/while/body/eval_jaxpr/ppermute | solution.py:21
  402.2 14.3 %collective-permute-done = f32[6,8,1024]{2,1,0:T(8,128)S(1)} collective-permute-done((f32[6,8,1024]{2,1,0:T(8,128)S(1)}, f32[6,8,1024]{2,1,0:T(8,128)S(1)}, u32[]{:S(2)}, u32[]{:S(2)}) %collective-permute-start) | collective-permute-done | bytes 196640 | tf_op jit(solution)/shard_map/while/body/eval_jaxpr/ppermute | solution.py:21
  419.4 14.3 %collective-permute-done = f32[6,8,1024]{2,1,0:T(8,128)S(1)} collective-permute-done((f32[6,8,1024]{2,1,0:T(8,128)S(1)}, f32[6,8,1024]{2,1,0:T(8,128)S(1)}, u32[]{:S(2)}, u32[]{:S(2)}) %collective-permute-start) | collective-permute-done | bytes 196640 | tf_op jit(solution)/shard_map/while/body/eval_jaxpr/ppermute | solution.py:21
  436.7 14.3 %collective-permute-done = f32[6,8,1024]{2,1,0:T(8,128)S(1)} collective-permute-done((f32[6,8,1024]{2,1,0:T(8,128)S(1)}, f32[6,8,1024]{2,1,0:T(8,128)S(1)}, u32[]{:S(2)}, u32[]{:S(2)}) %collective-permute-start) | collective-permute-done | bytes 196640 | tf_op jit(solution)/shard_map/while/body/eval_jaxpr/ppermute | solution.py:21
  453.9 14.3 %collective-permute-done = f32[6,8,1024]{2,1,0:T(8,128)S(1)} collective-permute-done((f32[6,8,1024]{2,1,0:T(8,128)S(1)}, f32[6,8,1024]{2,1,0:T(8,128)S(1)}, u32[]{:S(2)}, u32[]{:S(2)}) %collective-permute-start) | collective-permute-done | bytes 196640 | tf_op jit(solution)/shard_map/while/body/eval_jaxpr/ppermute | solution.py:21
  471.2 14.3 %collective-permute-done = f32[6,8,1024]{2,1,0:T(8,128)S(1)} collective-permute-done((f32[6,8,1024]{2,1,0:T(8,128)S(1)}, f32[6,8,1024]{2,1,0:T(8,128)S(1)}, u32[]{:S(2)}, u32[]{:S(2)}) %collective-permute-start) | collective-permute-done | bytes 196640 | tf_op jit(solution)/shard_map/while/body/eval_jaxpr/ppermute | solution.py:21
  488.4 14.3 %collective-permute-done = f32[6,8,1024]{2,1,0:T(8,128)S(1)} collective-permute-done((f32[6,8,1024]{2,1,0:T(8,128)S(1)}, f32[6,8,1024]{2,1,0:T(8,128)S(1)}, u32[]{:S(2)}, u32[]{:S(2)}) %collective-permute-start) | collective-permute-done | bytes 196640 | tf_op jit(solution)/shard_map/while/body/eval_jaxpr/ppermute | solution.py:21
  505.7 14.3 %collective-permute-done = f32[6,8,1024]{2,1,0:T(8,128)S(1)} collective-permute-done((f32[6,8,1024]{2,1,0:T(8,128)S(1)}, f32[6,8,1024]{2,1,0:T(8,128)S(1)}, u32[]{:S(2)}, u32[]{:S(2)}) %collective-permute-start) | collective-permute-done | bytes 196640 | tf_op jit(solution)/shard_map/while/body/eval_jaxpr/ppermute | solution.py:21
  522.9 14.3 %collective-permute-done = f32[6,8,1024]{2,1,0:T(8,128)S(1)} collective-permute-done((f32[6,8,1024]{2,1,0:T(8,128)S(1)}, f32[6,8,1024]{2,1,0:T(8,128)S(1)}, u32[]{:S(2)}, u32[]{:S(2)}) %collective-permute-start) | collective-permute-done | bytes 196640 | tf_op jit(solution)/shard_map/while/body/eval_jaxpr/ppermute | solution.py:21
  540.2 14.3 %collective-permute-done = f32[6,8,1024]{2,1,0:T(8,128)S(1)} collective-permute-done((f32[6,8,1024]{2,1,0:T(8,128)S(1)}, f32[6,8,1024]{2,1,0:T(8,128)S(1)}, u32[]{:S(2)}, u32[]{:S(2)}) %collective-permute-start) | collective-permute-done | bytes 196640 | tf_op jit(solution)/shard_map/while/body/eval_jaxpr/ppermute | solution.py:21
  557.4 15.2 %collective-permute-done = f32[6,8,1024]{2,1,0:T(8,128)S(1)} collective-permute-done((f32[6,8,1024]{2,1,0:T(8,128)S(1)}, f32[6,8,1024]{2,1,0:T(8,128)S(1)}, u32[]{:S(2)}, u32[]{:S(2)}) %collective-permute-start) | collective-permute-done | bytes 196640 | tf_op jit(solution)/shard_map/while/body/eval_jaxpr/ppermute | solution.py:21
  575.5 16.3 %collective-permute-done = f32[6,8,1024]{2,1,0:T(8,128)S(1)} collective-permute-done((f32[6,8,1024]{2,1,0:T(8,128)S(1)}, f32[6,8,1024]{2,1,0:T(8,128)S(1)}, u32[]{:S(2)}, u32[]{:S(2)}) %collective-permute-start) | collective-permute-done | bytes 196640 | tf_op jit(solution)/shard_map/while/body/eval_jaxpr/ppermute | solution.py:21
  594.7 15.6 %collective-permute-done = f32[6,8,1024]{2,1,0:T(8,128)S(1)} collective-permute-done((f32[6,8,1024]{2,1,0:T(8,128)S(1)}, f32[6,8,1024]{2,1,0:T(8,128)S(1)}, u32[]{:S(2)}, u32[]{:S(2)}) %collective-permute-start) | collective-permute-done | bytes 196640 | tf_op jit(solution)/shard_map/while/body/eval_jaxpr/ppermute | solution.py:21
  613.2 14.7 %collective-permute-done = f32[6,8,1024]{2,1,0:T(8,128)S(1)} collective-permute-done((f32[6,8,1024]{2,1,0:T(8,128)S(1)}, f32[6,8,1024]{2,1,0:T(8,128)S(1)}, u32[]{:S(2)}, u32[]{:S(2)}) %collective-permute-start) | collective-permute-done | bytes 196640 | tf_op jit(solution)/shard_map/while/body/eval_jaxpr/ppermute | solution.py:21
  630.9 14.3 %collective-permute-done = f32[6,8,1024]{2,1,0:T(8,128)S(1)} collective-permute-done((f32[6,8,1024]{2,1,0:T(8,128)S(1)}, f32[6,8,1024]{2,1,0:T(8,128)S(1)}, u32[]{:S(2)}, u32[]{:S(2)}) %collective-permute-start) | collective-permute-done | bytes 196640 | tf_op jit(solution)/shard_map/while/body/eval_jaxpr/ppermute | solution.py:21
  648.1 14.3 %collective-permute-done = f32[6,8,1024]{2,1,0:T(8,128)S(1)} collective-permute-done((f32[6,8,1024]{2,1,0:T(8,128)S(1)}, f32[6,8,1024]{2,1,0:T(8,128)S(1)}, u32[]{:S(2)}, u32[]{:S(2)}) %collective-permute-start) | collective-permute-done | bytes 196640 | tf_op jit(solution)/shard_map/while/body/eval_jaxpr/ppermute | solution.py:21
  665.3 14.3 %collective-permute-done = f32[6,8,1024]{2,1,0:T(8,128)S(1)} collective-permute-done((f32[6,8,1024]{2,1,0:T(8,128)S(1)}, f32[6,8,1024]{2,1,0:T(8,128)S(1)}, u32[]{:S(2)}, u32[]{:S(2)}) %collective-permute-start) | collective-permute-done | bytes 196640 | tf_op jit(solution)/shard_map/while/body/eval_jaxpr/ppermute | solution.py:21
  682.6 14.3 %collective-permute-done = f32[6,8,1024]{2,1,0:T(8,128)S(1)} collective-permute-done((f32[6,8,1024]{2,1,0:T(8,128)S(1)}, f32[6,8,1024]{2,1,0:T(8,128)S(1)}, u32[]{:S(2)}, u32[]{:S(2)}) %collective-permute-start) | collective-permute-done | bytes 196640 | tf_op jit(solution)/shard_map/while/body/eval_jaxpr/ppermute | solution.py:21
  699.8 14.3 %collective-permute-done = f32[6,8,1024]{2,1,0:T(8,128)S(1)} collective-permute-done((f32[6,8,1024]{2,1,0:T(8,128)S(1)}, f32[6,8,1024]{2,1,0:T(8,128)S(1)}, u32[]{:S(2)}, u32[]{:S(2)}) %collective-permute-start) | collective-permute-done | bytes 196640 | tf_op jit(solution)/shard_map/while/body/eval_jaxpr/ppermute | solution.py:21
  717.1 14.3 %collective-permute-done = f32[6,8,1024]{2,1,0:T(8,128)S(1)} collective-permute-done((f32[6,8,1024]{2,1,0:T(8,128)S(1)}, f32[6,8,1024]{2,1,0:T(8,128)S(1)}, u32[]{:S(2)}, u32[]{:S(2)}) %collective-permute-start) | collective-permute-done | bytes 196640 | tf_op jit(solution)/shard_map/while/body/eval_jaxpr/ppermute | solution.py:21
  734.3 14.3 %collective-permute-done = f32[6,8,1024]{2,1,0:T(8,128)S(1)} collective-permute-done((f32[6,8,1024]{2,1,0:T(8,128)S(1)}, f32[6,8,1024]{2,1,0:T(8,128)S(1)}, u32[]{:S(2)}, u32[]{:S(2)}) %collective-permute-start) | collective-permute-done | bytes 196640 | tf_op jit(solution)/shard_map/while/body/eval_jaxpr/ppermute | solution.py:21
  751.6 14.3 %collective-permute-done = f32[6,8,1024]{2,1,0:T(8,128)S(1)} collective-permute-done((f32[6,8,1024]{2,1,0:T(8,128)S(1)}, f32[6,8,1024]{2,1,0:T(8,128)S(1)}, u32[]{:S(2)}, u32[]{:S(2)}) %collective-permute-start) | collective-permute-done | bytes 196640 | tf_op jit(solution)/shard_map/while/body/eval_jaxpr/ppermute | solution.py:21
  768.8 14.3 %collective-permute-done = f32[6,8,1024]{2,1,0:T(8,128)S(1)} collective-permute-done((f32[6,8,1024]{2,1,0:T(8,128)S(1)}, f32[6,8,1024]{2,1,0:T(8,128)S(1)}, u32[]{:S(2)}, u32[]{:S(2)}) %collective-permute-start) | collective-permute-done | bytes 196640 | tf_op jit(solution)/shard_map/while/body/eval_jaxpr/ppermute | solution.py:21
  786.1 14.3 %collective-permute-done = f32[6,8,1024]{2,1,0:T(8,128)S(1)} collective-permute-done((f32[6,8,1024]{2,1,0:T(8,128)S(1)}, f32[6,8,1024]{2,1,0:T(8,128)S(1)}, u32[]{:S(2)}, u32[]{:S(2)}) %collective-permute-start) | collective-permute-done | bytes 196640 | tf_op jit(solution)/shard_map/while/body/eval_jaxpr/ppermute | solution.py:21
  803.3 14.4 %collective-permute-done = f32[6,8,1024]{2,1,0:T(8,128)S(1)} collective-permute-done((f32[6,8,1024]{2,1,0:T(8,128)S(1)}, f32[6,8,1024]{2,1,0:T(8,128)S(1)}, u32[]{:S(2)}, u32[]{:S(2)}) %collective-permute-start) | collective-permute-done | bytes 196640 | tf_op jit(solution)/shard_map/while/body/eval_jaxpr/ppermute | solution.py:21
  820.6 15.5 %collective-permute-done = f32[6,8,1024]{2,1,0:T(8,128)S(1)} collective-permute-done((f32[6,8,1024]{2,1,0:T(8,128)S(1)}, f32[6,8,1024]{2,1,0:T(8,128)S(1)}, u32[]{:S(2)}, u32[]{:S(2)}) %collective-permute-start) | collective-permute-done | bytes 196640 | tf_op jit(solution)/shard_map/while/body/eval_jaxpr/ppermute | solution.py:21
  839.1 14.3 %collective-permute-done = f32[6,8,1024]{2,1,0:T(8,128)S(1)} collective-permute-done((f32[6,8,1024]{2,1,0:T(8,128)S(1)}, f32[6,8,1024]{2,1,0:T(8,128)S(1)}, u32[]{:S(2)}, u32[]{:S(2)}) %collective-permute-start) | collective-permute-done | bytes 196640 | tf_op jit(solution)/shard_map/while/body/eval_jaxpr/ppermute | solution.py:21
  856.3 14.3 %collective-permute-done = f32[6,8,1024]{2,1,0:T(8,128)S(1)} collective-permute-done((f32[6,8,1024]{2,1,0:T(8,128)S(1)}, f32[6,8,1024]{2,1,0:T(8,128)S(1)}, u32[]{:S(2)}, u32[]{:S(2)}) %collective-permute-start) | collective-permute-done | bytes 196640 | tf_op jit(solution)/shard_map/while/body/eval_jaxpr/ppermute | solution.py:21
  (157 shorter events, 140.3 us)
Async XLA Ops:
  7.2 242.1 %all-gather.2.cloned.1.call-start = ((), (), s32[]{:S(2)}) async-start(), calls=%async_computation | async-start | bytes 3244032 | tf_op jit(solution)/shard_map/all_gather | solution.py:46
  9.6 247.5 %collective-permute-start.4 = (bf16[128,512]{0,1:T(8,128)(2,1)}, bf16[128,512]{0,1:T(8,128)(2,1)}, u32[]{:S(2)}, u32[]{:S(2)}) collective-permute-start(bf16[128,512]{0,1:T(8,128)(2,1)} %copy.43), channel_id=1, source_target_pairs={{0,8},{8,0},{1,9},{9,1},{2,10},{10,2},{3,11},{11,3},{4,12},{12,4},... | collective-permute-start | bytes 393224 | tf_op jit(solution)/shard_map/ppermute | solution.py:16
  25.3 233.0 %collective-permute-start.3 = (bf16[128,512]{0,1:T(8,128)(2,1)}, bf16[128,512]{0,1:T(8,128)(2,1)}, u32[]{:S(2)}, u32[]{:S(2)}) collective-permute-start(bf16[128,512]{0,1:T(8,128)(2,1)} %copy.43), channel_id=1, source_target_pairs={{0,4},{4,0},{1,5},{5,1},{2,6},{6,2},{3,7},{7,3},{8,12},{12,8},{9,1... | collective-permute-start | bytes 393224 | tf_op jit(solution)/shard_map/ppermute | solution.py:16
  29.5 230.0 %collective-permute-start.2 = (bf16[128,512]{0,1:T(8,128)(2,1)}, bf16[128,512]{0,1:T(8,128)(2,1)}, u32[]{:S(2)}, u32[]{:S(2)}) collective-permute-start(bf16[128,512]{0,1:T(8,128)(2,1)} %copy.43), channel_id=1, source_target_pairs={{0,2},{2,0},{1,3},{3,1},{4,6},{6,4},{5,7},{7,5},{8,10},{10,8},{9,1... | collective-permute-start | bytes 393224 | tf_op jit(solution)/shard_map/ppermute | solution.py:16
  32.8 228.0 %collective-permute-start.1 = (bf16[128,512]{0,1:T(8,128)(2,1)}, bf16[128,512]{0,1:T(8,128)(2,1)}, u32[]{:S(2)}, u32[]{:S(2)}) collective-permute-start(bf16[128,512]{0,1:T(8,128)(2,1)} %copy.43), channel_id=1, source_target_pairs={{0,1},{1,0},{2,3},{3,2},{4,5},{5,4},{6,7},{7,6},{8,9},{9,8},{10,11... | collective-permute-start | bytes 393224 | tf_op jit(solution)/shard_map/ppermute | solution.py:16
  38.6 214.7 %copy-start.7 = (bf16[128,1,2,1,256]{4,0,2,3,1:T(8,128)(2,1)}, bf16[128,1,2,1,256]{4,0,2,3,1:T(8,128)(2,1)S(1)}, u32[]{:S(2)}) copy-start(bf16[128,1,2,1,256]{4,0,2,3,1:T(8,128)(2,1)S(1)} %rev.4) | copy-start | bytes 393220
  249.2 3.7 copy-start.6
  257.0 9.1 %copy-start.5 = (bf16[1,256,1024]{1,2,0:T(8,128)(2,1)S(1)}, bf16[1,256,1024]{1,2,0:T(8,128)(2,1)}, u32[]{:S(2)}) copy-start(bf16[1,256,1024]{1,2,0:T(8,128)(2,1)} %copy.42) | copy-start | bytes 1572868
  258.3 10.1 %copy-start.8 = (bf16[128,1,2,1,256]{4,0,2,3,1:T(8,128)(2,1)S(1)}, bf16[128,1,2,1,256]{4,0,2,3,1:T(8,128)(2,1)}, u32[]{:S(2)}) copy-start(bf16[128,1,2,1,256]{4,0,2,3,1:T(8,128)(2,1)} %copy-done.7) | copy-start | bytes 393220
  276.4 596.2 %collective-permute-start.8 = (f32[128,512]{0,1:T(8,128)}, f32[128,512]{0,1:T(8,128)S(1)}, u32[]{:S(2)}, u32[]{:S(2)}) collective-permute-start(f32[128,512]{0,1:T(8,128)} %bitcast.26), channel_id=1, source_target_pairs={{0,8},{8,0},{1,9},{9,1},{2,10},{10,2},{3,11},{11,3},{4,12},{12,4},... | collective-permute-start | bytes 786440 | tf_op jit(solution)/shard_map/ppermute | solution.py:16
  282.1 590.6 %collective-permute-start.7 = (f32[128,512]{0,1:T(8,128)}, f32[128,512]{0,1:T(8,128)}, u32[]{:S(2)}, u32[]{:S(2)}) collective-permute-start(f32[128,512]{0,1:T(8,128)} %bitcast.23), channel_id=1, source_target_pairs={{0,4},{4,0},{1,5},{5,1},{2,6},{6,2},{3,7},{7,3},{8,12},{12,8},{9,1... | collective-permute-start | bytes 786440 | tf_op jit(solution)/shard_map/ppermute | solution.py:16
  288.1 584.6 %collective-permute-start.6 = (f32[128,512]{0,1:T(8,128)}, f32[128,512]{0,1:T(8,128)}, u32[]{:S(2)}, u32[]{:S(2)}) collective-permute-start(f32[128,512]{0,1:T(8,128)} %bitcast.20), channel_id=1, source_target_pairs={{0,2},{2,0},{1,3},{3,1},{4,6},{6,4},{5,7},{7,5},{8,10},{10,8},{9,1... | collective-permute-start | bytes 786440 | tf_op jit(solution)/shard_map/ppermute | solution.py:16
  291.4 581.3 %collective-permute-start.5 = (f32[128,512]{0,1:T(8,128)}, f32[128,512]{0,1:T(8,128)}, u32[]{:S(2)}, u32[]{:S(2)}) collective-permute-start(f32[128,512]{0,1:T(8,128)} %bitcast.17), channel_id=1, source_target_pairs={{0,1},{1,0},{2,3},{3,2},{4,5},{5,4},{6,7},{7,6},{8,9},{9,8},{10,11... | collective-permute-start | bytes 786440 | tf_op jit(solution)/shard_map/ppermute | solution.py:16
  316.2 7.7 copy-start
  319.4 6.5 copy-start.11
  320.7 4.9 copy-start.1
  320.7 5.3 copy-start.10
  328.9 17.9 %collective-permute-start = (f32[6,8,1024]{2,1,0:T(8,128)S(1)}, f32[6,8,1024]{2,1,0:T(8,128)S(1)}, u32[]{:S(2)}, u32[]{:S(2)}) collective-permute-start(f32[6,8,1024]{2,1,0:T(8,128)S(1)} %get-tuple-element.217), channel_id=1, source_target_pairs={{0,16},{16,32},{32,48},{48,64},{64,80},{80,96},{96,112},{112,128},... | collective-permute-start | bytes 589832 | tf_op jit(solution)/shard_map/while/body/eval_jaxpr/ppermute | solution.py:21
  347.7 17.1 %collective-permute-start = (f32[6,8,1024]{2,1,0:T(8,128)S(1)}, f32[6,8,1024]{2,1,0:T(8,128)S(1)}, u32[]{:S(2)}, u32[]{:S(2)}) collective-permute-start(f32[6,8,1024]{2,1,0:T(8,128)S(1)} %get-tuple-element.217), channel_id=1, source_target_pairs={{0,16},{16,32},{32,48},{48,64},{64,80},{80,96},{96,112},{112,128},... | collective-permute-start | bytes 589832 | tf_op jit(solution)/shard_map/while/body/eval_jaxpr/ppermute | solution.py:21
  365.8 16.3 %collective-permute-start = (f32[6,8,1024]{2,1,0:T(8,128)S(1)}, f32[6,8,1024]{2,1,0:T(8,128)S(1)}, u32[]{:S(2)}, u32[]{:S(2)}) collective-permute-start(f32[6,8,1024]{2,1,0:T(8,128)S(1)} %get-tuple-element.217), channel_id=1, source_target_pairs={{0,16},{16,32},{32,48},{48,64},{64,80},{80,96},{96,112},{112,128},... | collective-permute-start | bytes 589832 | tf_op jit(solution)/shard_map/while/body/eval_jaxpr/ppermute | solution.py:21
  383.0 16.3 %collective-permute-start = (f32[6,8,1024]{2,1,0:T(8,128)S(1)}, f32[6,8,1024]{2,1,0:T(8,128)S(1)}, u32[]{:S(2)}, u32[]{:S(2)}) collective-permute-start(f32[6,8,1024]{2,1,0:T(8,128)S(1)} %get-tuple-element.217), channel_id=1, source_target_pairs={{0,16},{16,32},{32,48},{48,64},{64,80},{80,96},{96,112},{112,128},... | collective-permute-start | bytes 589832 | tf_op jit(solution)/shard_map/while/body/eval_jaxpr/ppermute | solution.py:21
  400.3 16.3 %collective-permute-start = (f32[6,8,1024]{2,1,0:T(8,128)S(1)}, f32[6,8,1024]{2,1,0:T(8,128)S(1)}, u32[]{:S(2)}, u32[]{:S(2)}) collective-permute-start(f32[6,8,1024]{2,1,0:T(8,128)S(1)} %get-tuple-element.217), channel_id=1, source_target_pairs={{0,16},{16,32},{32,48},{48,64},{64,80},{80,96},{96,112},{112,128},... | collective-permute-start | bytes 589832 | tf_op jit(solution)/shard_map/while/body/eval_jaxpr/ppermute | solution.py:21
  417.5 16.3 %collective-permute-start = (f32[6,8,1024]{2,1,0:T(8,128)S(1)}, f32[6,8,1024]{2,1,0:T(8,128)S(1)}, u32[]{:S(2)}, u32[]{:S(2)}) collective-permute-start(f32[6,8,1024]{2,1,0:T(8,128)S(1)} %get-tuple-element.217), channel_id=1, source_target_pairs={{0,16},{16,32},{32,48},{48,64},{64,80},{80,96},{96,112},{112,128},... | collective-permute-start | bytes 589832 | tf_op jit(solution)/shard_map/while/body/eval_jaxpr/ppermute | solution.py:21
  434.7 16.3 %collective-permute-start = (f32[6,8,1024]{2,1,0:T(8,128)S(1)}, f32[6,8,1024]{2,1,0:T(8,128)S(1)}, u32[]{:S(2)}, u32[]{:S(2)}) collective-permute-start(f32[6,8,1024]{2,1,0:T(8,128)S(1)} %get-tuple-element.217), channel_id=1, source_target_pairs={{0,16},{16,32},{32,48},{48,64},{64,80},{80,96},{96,112},{112,128},... | collective-permute-start | bytes 589832 | tf_op jit(solution)/shard_map/while/body/eval_jaxpr/ppermute | solution.py:21
  452.0 16.3 %collective-permute-start = (f32[6,8,1024]{2,1,0:T(8,128)S(1)}, f32[6,8,1024]{2,1,0:T(8,128)S(1)}, u32[]{:S(2)}, u32[]{:S(2)}) collective-permute-start(f32[6,8,1024]{2,1,0:T(8,128)S(1)} %get-tuple-element.217), channel_id=1, source_target_pairs={{0,16},{16,32},{32,48},{48,64},{64,80},{80,96},{96,112},{112,128},... | collective-permute-start | bytes 589832 | tf_op jit(solution)/shard_map/while/body/eval_jaxpr/ppermute | solution.py:21
  469.2 16.3 %collective-permute-start = (f32[6,8,1024]{2,1,0:T(8,128)S(1)}, f32[6,8,1024]{2,1,0:T(8,128)S(1)}, u32[]{:S(2)}, u32[]{:S(2)}) collective-permute-start(f32[6,8,1024]{2,1,0:T(8,128)S(1)} %get-tuple-element.217), channel_id=1, source_target_pairs={{0,16},{16,32},{32,48},{48,64},{64,80},{80,96},{96,112},{112,128},... | collective-permute-start | bytes 589832 | tf_op jit(solution)/shard_map/while/body/eval_jaxpr/ppermute | solution.py:21
  486.5 16.3 %collective-permute-start = (f32[6,8,1024]{2,1,0:T(8,128)S(1)}, f32[6,8,1024]{2,1,0:T(8,128)S(1)}, u32[]{:S(2)}, u32[]{:S(2)}) collective-permute-start(f32[6,8,1024]{2,1,0:T(8,128)S(1)} %get-tuple-element.217), channel_id=1, source_target_pairs={{0,16},{16,32},{32,48},{48,64},{64,80},{80,96},{96,112},{112,128},... | collective-permute-start | bytes 589832 | tf_op jit(solution)/shard_map/while/body/eval_jaxpr/ppermute | solution.py:21
  503.7 16.3 %collective-permute-start = (f32[6,8,1024]{2,1,0:T(8,128)S(1)}, f32[6,8,1024]{2,1,0:T(8,128)S(1)}, u32[]{:S(2)}, u32[]{:S(2)}) collective-permute-start(f32[6,8,1024]{2,1,0:T(8,128)S(1)} %get-tuple-element.217), channel_id=1, source_target_pairs={{0,16},{16,32},{32,48},{48,64},{64,80},{80,96},{96,112},{112,128},... | collective-permute-start | bytes 589832 | tf_op jit(solution)/shard_map/while/body/eval_jaxpr/ppermute | solution.py:21
  521.0 16.3 %collective-permute-start = (f32[6,8,1024]{2,1,0:T(8,128)S(1)}, f32[6,8,1024]{2,1,0:T(8,128)S(1)}, u32[]{:S(2)}, u32[]{:S(2)}) collective-permute-start(f32[6,8,1024]{2,1,0:T(8,128)S(1)} %get-tuple-element.217), channel_id=1, source_target_pairs={{0,16},{16,32},{32,48},{48,64},{64,80},{80,96},{96,112},{112,128},... | collective-permute-start | bytes 589832 | tf_op jit(solution)/shard_map/while/body/eval_jaxpr/ppermute | solution.py:21
  538.2 16.3 %collective-permute-start = (f32[6,8,1024]{2,1,0:T(8,128)S(1)}, f32[6,8,1024]{2,1,0:T(8,128)S(1)}, u32[]{:S(2)}, u32[]{:S(2)}) collective-permute-start(f32[6,8,1024]{2,1,0:T(8,128)S(1)} %get-tuple-element.217), channel_id=1, source_target_pairs={{0,16},{16,32},{32,48},{48,64},{64,80},{80,96},{96,112},{112,128},... | collective-permute-start | bytes 589832 | tf_op jit(solution)/shard_map/while/body/eval_jaxpr/ppermute | solution.py:21
  555.5 17.1 %collective-permute-start = (f32[6,8,1024]{2,1,0:T(8,128)S(1)}, f32[6,8,1024]{2,1,0:T(8,128)S(1)}, u32[]{:S(2)}, u32[]{:S(2)}) collective-permute-start(f32[6,8,1024]{2,1,0:T(8,128)S(1)} %get-tuple-element.217), channel_id=1, source_target_pairs={{0,16},{16,32},{32,48},{48,64},{64,80},{80,96},{96,112},{112,128},... | collective-permute-start | bytes 589832 | tf_op jit(solution)/shard_map/while/body/eval_jaxpr/ppermute | solution.py:21
  573.5 18.3 %collective-permute-start = (f32[6,8,1024]{2,1,0:T(8,128)S(1)}, f32[6,8,1024]{2,1,0:T(8,128)S(1)}, u32[]{:S(2)}, u32[]{:S(2)}) collective-permute-start(f32[6,8,1024]{2,1,0:T(8,128)S(1)} %get-tuple-element.217), channel_id=1, source_target_pairs={{0,16},{16,32},{32,48},{48,64},{64,80},{80,96},{96,112},{112,128},... | collective-permute-start | bytes 589832 | tf_op jit(solution)/shard_map/while/body/eval_jaxpr/ppermute | solution.py:21
  592.8 17.5 %collective-permute-start = (f32[6,8,1024]{2,1,0:T(8,128)S(1)}, f32[6,8,1024]{2,1,0:T(8,128)S(1)}, u32[]{:S(2)}, u32[]{:S(2)}) collective-permute-start(f32[6,8,1024]{2,1,0:T(8,128)S(1)} %get-tuple-element.217), channel_id=1, source_target_pairs={{0,16},{16,32},{32,48},{48,64},{64,80},{80,96},{96,112},{112,128},... | collective-permute-start | bytes 589832 | tf_op jit(solution)/shard_map/while/body/eval_jaxpr/ppermute | solution.py:21
  611.3 16.7 %collective-permute-start = (f32[6,8,1024]{2,1,0:T(8,128)S(1)}, f32[6,8,1024]{2,1,0:T(8,128)S(1)}, u32[]{:S(2)}, u32[]{:S(2)}) collective-permute-start(f32[6,8,1024]{2,1,0:T(8,128)S(1)} %get-tuple-element.217), channel_id=1, source_target_pairs={{0,16},{16,32},{32,48},{48,64},{64,80},{80,96},{96,112},{112,128},... | collective-permute-start | bytes 589832 | tf_op jit(solution)/shard_map/while/body/eval_jaxpr/ppermute | solution.py:21
  628.9 16.3 %collective-permute-start = (f32[6,8,1024]{2,1,0:T(8,128)S(1)}, f32[6,8,1024]{2,1,0:T(8,128)S(1)}, u32[]{:S(2)}, u32[]{:S(2)}) collective-permute-start(f32[6,8,1024]{2,1,0:T(8,128)S(1)} %get-tuple-element.217), channel_id=1, source_target_pairs={{0,16},{16,32},{32,48},{48,64},{64,80},{80,96},{96,112},{112,128},... | collective-permute-start | bytes 589832 | tf_op jit(solution)/shard_map/while/body/eval_jaxpr/ppermute | solution.py:21
  646.2 16.3 %collective-permute-start = (f32[6,8,1024]{2,1,0:T(8,128)S(1)}, f32[6,8,1024]{2,1,0:T(8,128)S(1)}, u32[]{:S(2)}, u32[]{:S(2)}) collective-permute-start(f32[6,8,1024]{2,1,0:T(8,128)S(1)} %get-tuple-element.217), channel_id=1, source_target_pairs={{0,16},{16,32},{32,48},{48,64},{64,80},{80,96},{96,112},{112,128},... | collective-permute-start | bytes 589832 | tf_op jit(solution)/shard_map/while/body/eval_jaxpr/ppermute | solution.py:21
  663.4 16.3 %collective-permute-start = (f32[6,8,1024]{2,1,0:T(8,128)S(1)}, f32[6,8,1024]{2,1,0:T(8,128)S(1)}, u32[]{:S(2)}, u32[]{:S(2)}) collective-permute-start(f32[6,8,1024]{2,1,0:T(8,128)S(1)} %get-tuple-element.217), channel_id=1, source_target_pairs={{0,16},{16,32},{32,48},{48,64},{64,80},{80,96},{96,112},{112,128},... | collective-permute-start | bytes 589832 | tf_op jit(solution)/shard_map/while/body/eval_jaxpr/ppermute | solution.py:21
  680.6 16.3 %collective-permute-start = (f32[6,8,1024]{2,1,0:T(8,128)S(1)}, f32[6,8,1024]{2,1,0:T(8,128)S(1)}, u32[]{:S(2)}, u32[]{:S(2)}) collective-permute-start(f32[6,8,1024]{2,1,0:T(8,128)S(1)} %get-tuple-element.217), channel_id=1, source_target_pairs={{0,16},{16,32},{32,48},{48,64},{64,80},{80,96},{96,112},{112,128},... | collective-permute-start | bytes 589832 | tf_op jit(solution)/shard_map/while/body/eval_jaxpr/ppermute | solution.py:21
  697.9 16.3 %collective-permute-start = (f32[6,8,1024]{2,1,0:T(8,128)S(1)}, f32[6,8,1024]{2,1,0:T(8,128)S(1)}, u32[]{:S(2)}, u32[]{:S(2)}) collective-permute-start(f32[6,8,1024]{2,1,0:T(8,128)S(1)} %get-tuple-element.217), channel_id=1, source_target_pairs={{0,16},{16,32},{32,48},{48,64},{64,80},{80,96},{96,112},{112,128},... | collective-permute-start | bytes 589832 | tf_op jit(solution)/shard_map/while/body/eval_jaxpr/ppermute | solution.py:21
  715.1 16.3 %collective-permute-start = (f32[6,8,1024]{2,1,0:T(8,128)S(1)}, f32[6,8,1024]{2,1,0:T(8,128)S(1)}, u32[]{:S(2)}, u32[]{:S(2)}) collective-permute-start(f32[6,8,1024]{2,1,0:T(8,128)S(1)} %get-tuple-element.217), channel_id=1, source_target_pairs={{0,16},{16,32},{32,48},{48,64},{64,80},{80,96},{96,112},{112,128},... | collective-permute-start | bytes 589832 | tf_op jit(solution)/shard_map/while/body/eval_jaxpr/ppermute | solution.py:21
  732.4 16.3 %collective-permute-start = (f32[6,8,1024]{2,1,0:T(8,128)S(1)}, f32[6,8,1024]{2,1,0:T(8,128)S(1)}, u32[]{:S(2)}, u32[]{:S(2)}) collective-permute-start(f32[6,8,1024]{2,1,0:T(8,128)S(1)} %get-tuple-element.217), channel_id=1, source_target_pairs={{0,16},{16,32},{32,48},{48,64},{64,80},{80,96},{96,112},{112,128},... | collective-permute-start | bytes 589832 | tf_op jit(solution)/shard_map/while/body/eval_jaxpr/ppermute | solution.py:21
  749.6 16.3 %collective-permute-start = (f32[6,8,1024]{2,1,0:T(8,128)S(1)}, f32[6,8,1024]{2,1,0:T(8,128)S(1)}, u32[]{:S(2)}, u32[]{:S(2)}) collective-permute-start(f32[6,8,1024]{2,1,0:T(8,128)S(1)} %get-tuple-element.217), channel_id=1, source_target_pairs={{0,16},{16,32},{32,48},{48,64},{64,80},{80,96},{96,112},{112,128},... | collective-permute-start | bytes 589832 | tf_op jit(solution)/shard_map/while/body/eval_jaxpr/ppermute | solution.py:21
  766.9 16.3 %collective-permute-start = (f32[6,8,1024]{2,1,0:T(8,128)S(1)}, f32[6,8,1024]{2,1,0:T(8,128)S(1)}, u32[]{:S(2)}, u32[]{:S(2)}) collective-permute-start(f32[6,8,1024]{2,1,0:T(8,128)S(1)} %get-tuple-element.217), channel_id=1, source_target_pairs={{0,16},{16,32},{32,48},{48,64},{64,80},{80,96},{96,112},{112,128},... | collective-permute-start | bytes 589832 | tf_op jit(solution)/shard_map/while/body/eval_jaxpr/ppermute | solution.py:21
  784.1 16.3 %collective-permute-start = (f32[6,8,1024]{2,1,0:T(8,128)S(1)}, f32[6,8,1024]{2,1,0:T(8,128)S(1)}, u32[]{:S(2)}, u32[]{:S(2)}) collective-permute-start(f32[6,8,1024]{2,1,0:T(8,128)S(1)} %get-tuple-element.217), channel_id=1, source_target_pairs={{0,16},{16,32},{32,48},{48,64},{64,80},{80,96},{96,112},{112,128},... | collective-permute-start | bytes 589832 | tf_op jit(solution)/shard_map/while/body/eval_jaxpr/ppermute | solution.py:21
  801.4 16.3 %collective-permute-start = (f32[6,8,1024]{2,1,0:T(8,128)S(1)}, f32[6,8,1024]{2,1,0:T(8,128)S(1)}, u32[]{:S(2)}, u32[]{:S(2)}) collective-permute-start(f32[6,8,1024]{2,1,0:T(8,128)S(1)} %get-tuple-element.217), channel_id=1, source_target_pairs={{0,16},{16,32},{32,48},{48,64},{64,80},{80,96},{96,112},{112,128},... | collective-permute-start | bytes 589832 | tf_op jit(solution)/shard_map/while/body/eval_jaxpr/ppermute | solution.py:21
  818.7 17.5 %collective-permute-start = (f32[6,8,1024]{2,1,0:T(8,128)S(1)}, f32[6,8,1024]{2,1,0:T(8,128)S(1)}, u32[]{:S(2)}, u32[]{:S(2)}) collective-permute-start(f32[6,8,1024]{2,1,0:T(8,128)S(1)} %get-tuple-element.217), channel_id=1, source_target_pairs={{0,16},{16,32},{32,48},{48,64},{64,80},{80,96},{96,112},{112,128},... | collective-permute-start | bytes 589832 | tf_op jit(solution)/shard_map/while/body/eval_jaxpr/ppermute | solution.py:21
  837.1 16.3 %collective-permute-start = (f32[6,8,1024]{2,1,0:T(8,128)S(1)}, f32[6,8,1024]{2,1,0:T(8,128)S(1)}, u32[]{:S(2)}, u32[]{:S(2)}) collective-permute-start(f32[6,8,1024]{2,1,0:T(8,128)S(1)} %get-tuple-element.217), channel_id=1, source_target_pairs={{0,16},{16,32},{32,48},{48,64},{64,80},{80,96},{96,112},{112,128},... | collective-permute-start | bytes 589832 | tf_op jit(solution)/shard_map/while/body/eval_jaxpr/ppermute | solution.py:21
  854.4 16.3 %collective-permute-start = (f32[6,8,1024]{2,1,0:T(8,128)S(1)}, f32[6,8,1024]{2,1,0:T(8,128)S(1)}, u32[]{:S(2)}, u32[]{:S(2)}) collective-permute-start(f32[6,8,1024]{2,1,0:T(8,128)S(1)} %get-tuple-element.217), channel_id=1, source_target_pairs={{0,16},{16,32},{32,48},{48,64},{64,80},{80,96},{96,112},{112,128},... | collective-permute-start | bytes 589832 | tf_op jit(solution)/shard_map/while/body/eval_jaxpr/ppermute | solution.py:21
  (4 other events, 8.6 us)
Sparse Core Ops, SparseCore 0:
  10.1 239.1 all-gather.1
where the time goes:
time: 884 us; the launch traced here: 882 us
  waiting for transfers between devices  662 us (75%)
  starting transfers between devices  102 us (12%)
  local copies, waits for them, and re-layouts  44.5 us (5%)
  other arithmetic  36.4 us (4%)
  matrix products  21 us (2%)
  between operations  14.4 us (2%)
    ppermute x31, waiting for transfers between devices, shifted(): lax.ppermute(value, axis, [(i, (i + by) % devices) for i in range(devices)])  452 us
    all_gather x1, waiting for transfers between devices, body(): weights = lax.all_gather(w_up, 'dp', axis=1, tiled=True)  209 us
    ppermute x31, starting transfers between devices, shifted(): lax.ppermute(value, axis, [(i, (i + by) % devices) for i in range(devices)])  59.5 us
    ppermute x8, starting transfers between devices, partner_2(): return lax.ppermute(block, axis, route)  42.1 us
    add x31, other arithmetic, turn_one(): shifted(carry, 'dp', 1)  29.4 us
    reshape x6, local copies, waits for them, and re-layouts, body(): product_term.reshape(BS, hidden_width) * keep_f[factor][None, :]  18.8 us
  transfers between devices with their start and end apart: 40, of which 32 were waited for; matrix products, arithmetic and copies ran while one was open for 9% of the time, Pallas kernels for 0%

commit v1 on v0

--- a/solution.py
+++ b/solution.py
@@ -43,7 +43,10 @@
     hidden_width = hidden_grad.shape[1]
     local_blocks = local_width // BS
     group_width = hidden_width // local_blocks
-    weights = lax.all_gather(w_up, "dp", axis=1, tiled=True)
+    frame_out = jax.lax.all_to_all(
+        jnp.stack([w_up for _ in range(jax.lax.axis_size("dp"))], 0), "dp", 0, 0
+    )
+    weights = jnp.concatenate(frame_out, axis=1)
     keep_cols = jnp.broadcast_to(pattern[:, :, None], (factor_count, pattern.shape[1], BS)).reshape(
         factor_count, hidden_width
     )

time: 884 us -> 800 us (0.905)
  waiting for transfers between devices: 662 us -> 579 us
  between operations: 14.4 us -> 1.07 us
  starting transfers between devices: 102 us -> 112 us
    all_gather x1 -> x0, waiting for transfers between devices: 209 us -> none  [body(): weights = lax.all_gather(w_up, 'dp', axis=1, tiled=True)]
    all_to_all x0 -> x1, waiting for transfers between devices: none -> 129 us  [body(): jax.lax.all_to_all(jnp.stack([w_up for _ in range(jax.lax.axis_size('dp')...]
    all_to_all x0 -> x1, starting transfers between devices: none -> 15.4 us  [body(): jax.lax.all_to_all(jnp.stack([w_up for _ in range(jax.lax.axis_size('dp')...]
  transfers between devices with their start and end apart: 40 -> 40, of which waited for: 32 -> 32; matrix products, arithmetic and copies ran while one was open for 9% -> 10% of each run, Pallas kernels for 0% -> 0%
where the time goes in v1:
time: 800 us; the launch traced here: 797 us
  waiting for transfers between devices  579 us (72%)
  starting transfers between devices  112 us (14%)
  local copies, waits for them, and re-layouts  47 us (6%)
  other arithmetic  34.4 us (4%)
  matrix products  22 us (3%)
    ppermute x31, waiting for transfers between devices, shifted(): lax.ppermute(value, axis, [(i, (i + by) % devices) for i in range(devices)])  451 us
    all_to_all x1, waiting for transfers between devices, body(): jax.lax.all_to_all(jnp.stack([w_up for _ in range(jax.lax.axis_size('dp')...  129 us
    ppermute x31, starting transfers between devices, shifted(): lax.ppermute(value, axis, [(i, (i + by) % devices) for i in range(devices)])  60.9 us
    ppermute x8, starting transfers between devices, partner_2(): return lax.ppermute(block, axis, route)  35.4 us
    add x31, other arithmetic, turn_one(): shifted(carry, 'dp', 1)  29.4 us
    reshape x6, local copies, waits for them, and re-layouts, body(): product_term.reshape(BS, hidden_width) * keep_f[factor][None, :]  18.8 us
  transfers between devices with their start and end apart: 40, of which 32 were waited for; matrix products, arithmetic and copies ran while one was open for 10% of the time, Pallas kernels for 0%

profile of v1, /device:TPU:8, one launch (start us, length us, event | category | flops | bytes accessed | tf_op | source)
XLA Modules:
  0.0 797.0 jit_solution(855160336017006752)
XLA Ops:
  0.6 2.9 stack.4
  3.6 15.4 %all-to-all-start = ((bf16[32,6,8,1024]{3,2,1,0:T(8,128)(2,1)}), bf16[32,6,8,1024]{3,2,1,0:T(8,128)(2,1)S(1)}, u32[]{:S(2)}, u32[]{:S(2)}) async-start(bf16[32,6,8,1024]{3,2,1,0:T(8,128)(2,1)} %stack.4), calls=%async_computation | async-start | bytes 6291456 | tf_op jit(solution)/shard_map/all_to_all | solution.py:46
  19.8 8.2 %collective-permute-start.4 = (bf16[128,512]{0,1:T(8,128)(2,1)}, bf16[128,512]{0,1:T(8,128)(2,1)}, u32[]{:S(2)}, u32[]{:S(2)}) collective-permute-start(bf16[128,512]{0,1:T(8,128)(2,1)} %copy.82), channel_id=1, source_target_pairs={{0,8},{8,0},{1,9},{9,1},{2,10},{10,2},{3,11},{11,3},{4,12},{12,4},... | collective-permute-start | bytes 393224 | tf_op jit(solution)/shard_map/ppermute | solution.py:16
  28.0 4.2 collective-permute-start.3
  32.2 3.3 collective-permute-start.2
  42.5 128.5 %all-to-all-done = bf16[32,6,8,1024]{3,2,1,0:T(8,128)(2,1)S(1)} async-done(((bf16[32,6,8,1024]{3,2,1,0:T(8,128)(2,1)}), bf16[32,6,8,1024]{3,2,1,0:T(8,128)(2,1)S(1)}, u32[]{:S(2)}, u32[]{:S(2)}) %all-to-all-start) | async-done | bytes 3145760 | tf_op jit(solution)/shard_map/all_to_all | solution.py:46
  198.0 8.2 %collective-permute-start.8 = (f32[128,512]{0,1:T(8,128)}, f32[128,512]{0,1:T(8,128)S(1)}, u32[]{:S(2)}, u32[]{:S(2)}) collective-permute-start(f32[128,512]{0,1:T(8,128)} %bitcast.28), channel_id=1, source_target_pairs={{0,8},{8,0},{1,9},{9,1},{2,10},{10,2},{3,11},{11,3},{4,12},{12,4},... | collective-permute-start | bytes 786440 | tf_op jit(solution)/shard_map/ppermute | solution.py:16
  206.2 4.2 collective-permute-start.7
  210.4 3.3 collective-permute-start.6
  218.1 3.1 reshape.273
  223.4 3.1 reshape.274
  228.8 3.1 reshape.275
  234.2 3.1 reshape.276
  238.6 3.2 reshape.277
  243.0 3.2 reshape.278
  251.2 542.7 %while.17 = (s32[]{:T(128)}, f32[6,8,1024]{2,1,0:T(8,128)S(1)}, s32[]{:T(128)}, f32[6,32,8,1024]{3,2,1,0:T(8,128)}, s32[]{:T(128)}, /*index=5*/s32[]{:T(128)}, s32[]{:T(128)}, s32[]{:T(128)}, s32[]{:T(128)}) while((s32[]{:T(128)}, f32[6,8,1024]{2,1,0:T(8,128)S(1)}, s32[]{:T(128)}, f32[6,32,8,1024]{3,2,1,0:T(8,128)}, s32[]{:T(128)}, ...), condition=%wide.region_1.2_spmd, body=%wide.region_0.1_spmd.sunk | while | flops 49170 | bytes 1376560 | solution.py:106
  251.2 3.3 collective-permute-start
  254.6 14.6 %collective-permute-done = f32[6,8,1024]{2,1,0:T(8,128)S(1)} collective-permute-done((f32[6,8,1024]{2,1,0:T(8,128)S(1)}, f32[6,8,1024]{2,1,0:T(8,128)S(1)}, u32[]{:S(2)}, u32[]{:S(2)}) %collective-permute-start) | collective-permute-done | bytes 196640 | tf_op jit(solution)/shard_map/while/body/eval_jaxpr/ppermute | solution.py:21
  272.0 15.1 %collective-permute-done = f32[6,8,1024]{2,1,0:T(8,128)S(1)} collective-permute-done((f32[6,8,1024]{2,1,0:T(8,128)S(1)}, f32[6,8,1024]{2,1,0:T(8,128)S(1)}, u32[]{:S(2)}, u32[]{:S(2)}) %collective-permute-start) | collective-permute-done | bytes 196640 | tf_op jit(solution)/shard_map/while/body/eval_jaxpr/ppermute | solution.py:21
  290.1 14.3 %collective-permute-done = f32[6,8,1024]{2,1,0:T(8,128)S(1)} collective-permute-done((f32[6,8,1024]{2,1,0:T(8,128)S(1)}, f32[6,8,1024]{2,1,0:T(8,128)S(1)}, u32[]{:S(2)}, u32[]{:S(2)}) %collective-permute-start) | collective-permute-done | bytes 196640 | tf_op jit(solution)/shard_map/while/body/eval_jaxpr/ppermute | solution.py:21
  307.3 14.3 %collective-permute-done = f32[6,8,1024]{2,1,0:T(8,128)S(1)} collective-permute-done((f32[6,8,1024]{2,1,0:T(8,128)S(1)}, f32[6,8,1024]{2,1,0:T(8,128)S(1)}, u32[]{:S(2)}, u32[]{:S(2)}) %collective-permute-start) | collective-permute-done | bytes 196640 | tf_op jit(solution)/shard_map/while/body/eval_jaxpr/ppermute | solution.py:21
  324.6 14.3 %collective-permute-done = f32[6,8,1024]{2,1,0:T(8,128)S(1)} collective-permute-done((f32[6,8,1024]{2,1,0:T(8,128)S(1)}, f32[6,8,1024]{2,1,0:T(8,128)S(1)}, u32[]{:S(2)}, u32[]{:S(2)}) %collective-permute-start) | collective-permute-done | bytes 196640 | tf_op jit(solution)/shard_map/while/body/eval_jaxpr/ppermute | solution.py:21
  341.8 14.3 %collective-permute-done = f32[6,8,1024]{2,1,0:T(8,128)S(1)} collective-permute-done((f32[6,8,1024]{2,1,0:T(8,128)S(1)}, f32[6,8,1024]{2,1,0:T(8,128)S(1)}, u32[]{:S(2)}, u32[]{:S(2)}) %collective-permute-start) | collective-permute-done | bytes 196640 | tf_op jit(solution)/shard_map/while/body/eval_jaxpr/ppermute | solution.py:21
  359.0 14.3 %collective-permute-done = f32[6,8,1024]{2,1,0:T(8,128)S(1)} collective-permute-done((f32[6,8,1024]{2,1,0:T(8,128)S(1)}, f32[6,8,1024]{2,1,0:T(8,128)S(1)}, u32[]{:S(2)}, u32[]{:S(2)}) %collective-permute-start) | collective-permute-done | bytes 196640 | tf_op jit(solution)/shard_map/while/body/eval_jaxpr/ppermute | solution.py:21
  376.3 14.3 %collective-permute-done = f32[6,8,1024]{2,1,0:T(8,128)S(1)} collective-permute-done((f32[6,8,1024]{2,1,0:T(8,128)S(1)}, f32[6,8,1024]{2,1,0:T(8,128)S(1)}, u32[]{:S(2)}, u32[]{:S(2)}) %collective-permute-start) | collective-permute-done | bytes 196640 | tf_op jit(solution)/shard_map/while/body/eval_jaxpr/ppermute | solution.py:21
  393.5 14.3 %collective-permute-done = f32[6,8,1024]{2,1,0:T(8,128)S(1)} collective-permute-done((f32[6,8,1024]{2,1,0:T(8,128)S(1)}, f32[6,8,1024]{2,1,0:T(8,128)S(1)}, u32[]{:S(2)}, u32[]{:S(2)}) %collective-permute-start) | collective-permute-done | bytes 196640 | tf_op jit(solution)/shard_map/while/body/eval_jaxpr/ppermute | solution.py:21
  410.8 14.3 %collective-permute-done = f32[6,8,1024]{2,1,0:T(8,128)S(1)} collective-permute-done((f32[6,8,1024]{2,1,0:T(8,128)S(1)}, f32[6,8,1024]{2,1,0:T(8,128)S(1)}, u32[]{:S(2)}, u32[]{:S(2)}) %collective-permute-start) | collective-permute-done | bytes 196640 | tf_op jit(solution)/shard_map/while/body/eval_jaxpr/ppermute | solution.py:21
  428.0 14.3 %collective-permute-done = f32[6,8,1024]{2,1,0:T(8,128)S(1)} collective-permute-done((f32[6,8,1024]{2,1,0:T(8,128)S(1)}, f32[6,8,1024]{2,1,0:T(8,128)S(1)}, u32[]{:S(2)}, u32[]{:S(2)}) %collective-permute-start) | collective-permute-done | bytes 196640 | tf_op jit(solution)/shard_map/while/body/eval_jaxpr/ppermute | solution.py:21
  445.3 14.3 %collective-permute-done = f32[6,8,1024]{2,1,0:T(8,128)S(1)} collective-permute-done((f32[6,8,1024]{2,1,0:T(8,128)S(1)}, f32[6,8,1024]{2,1,0:T(8,128)S(1)}, u32[]{:S(2)}, u32[]{:S(2)}) %collective-permute-start) | collective-permute-done | bytes 196640 | tf_op jit(solution)/shard_map/while/body/eval_jaxpr/ppermute | solution.py:21
  462.5 14.3 %collective-permute-done = f32[6,8,1024]{2,1,0:T(8,128)S(1)} collective-permute-done((f32[6,8,1024]{2,1,0:T(8,128)S(1)}, f32[6,8,1024]{2,1,0:T(8,128)S(1)}, u32[]{:S(2)}, u32[]{:S(2)}) %collective-permute-start) | collective-permute-done | bytes 196640 | tf_op jit(solution)/shard_map/while/body/eval_jaxpr/ppermute | solution.py:21
  479.8 15.2 %collective-permute-done = f32[6,8,1024]{2,1,0:T(8,128)S(1)} collective-permute-done((f32[6,8,1024]{2,1,0:T(8,128)S(1)}, f32[6,8,1024]{2,1,0:T(8,128)S(1)}, u32[]{:S(2)}, u32[]{:S(2)}) %collective-permute-start) | collective-permute-done | bytes 196640 | tf_op jit(solution)/shard_map/while/body/eval_jaxpr/ppermute | solution.py:21
  497.8 16.3 %collective-permute-done = f32[6,8,1024]{2,1,0:T(8,128)S(1)} collective-permute-done((f32[6,8,1024]{2,1,0:T(8,128)S(1)}, f32[6,8,1024]{2,1,0:T(8,128)S(1)}, u32[]{:S(2)}, u32[]{:S(2)}) %collective-permute-start) | collective-permute-done | bytes 196640 | tf_op jit(solution)/shard_map/while/body/eval_jaxpr/ppermute | solution.py:21
  517.1 15.6 %collective-permute-done = f32[6,8,1024]{2,1,0:T(8,128)S(1)} collective-permute-done((f32[6,8,1024]{2,1,0:T(8,128)S(1)}, f32[6,8,1024]{2,1,0:T(8,128)S(1)}, u32[]{:S(2)}, u32[]{:S(2)}) %collective-permute-start) | collective-permute-done | bytes 196640 | tf_op jit(solution)/shard_map/while/body/eval_jaxpr/ppermute | solution.py:21
  535.6 14.7 %collective-permute-done = f32[6,8,1024]{2,1,0:T(8,128)S(1)} collective-permute-done((f32[6,8,1024]{2,1,0:T(8,128)S(1)}, f32[6,8,1024]{2,1,0:T(8,128)S(1)}, u32[]{:S(2)}, u32[]{:S(2)}) %collective-permute-start) | collective-permute-done | bytes 196640 | tf_op jit(solution)/shard_map/while/body/eval_jaxpr/ppermute | solution.py:21
  553.2 14.3 %collective-permute-done = f32[6,8,1024]{2,1,0:T(8,128)S(1)} collective-permute-done((f32[6,8,1024]{2,1,0:T(8,128)S(1)}, f32[6,8,1024]{2,1,0:T(8,128)S(1)}, u32[]{:S(2)}, u32[]{:S(2)}) %collective-permute-start) | collective-permute-done | bytes 196640 | tf_op jit(solution)/shard_map/while/body/eval_jaxpr/ppermute | solution.py:21
  570.5 14.3 %collective-permute-done = f32[6,8,1024]{2,1,0:T(8,128)S(1)} collective-permute-done((f32[6,8,1024]{2,1,0:T(8,128)S(1)}, f32[6,8,1024]{2,1,0:T(8,128)S(1)}, u32[]{:S(2)}, u32[]{:S(2)}) %collective-permute-start) | collective-permute-done | bytes 196640 | tf_op jit(solution)/shard_map/while/body/eval_jaxpr/ppermute | solution.py:21
  587.7 14.3 %collective-permute-done = f32[6,8,1024]{2,1,0:T(8,128)S(1)} collective-permute-done((f32[6,8,1024]{2,1,0:T(8,128)S(1)}, f32[6,8,1024]{2,1,0:T(8,128)S(1)}, u32[]{:S(2)}, u32[]{:S(2)}) %collective-permute-start) | collective-permute-done | bytes 196640 | tf_op jit(solution)/shard_map/while/body/eval_jaxpr/ppermute | solution.py:21
  604.9 14.3 %collective-permute-done = f32[6,8,1024]{2,1,0:T(8,128)S(1)} collective-permute-done((f32[6,8,1024]{2,1,0:T(8,128)S(1)}, f32[6,8,1024]{2,1,0:T(8,128)S(1)}, u32[]{:S(2)}, u32[]{:S(2)}) %collective-permute-start) | collective-permute-done | bytes 196640 | tf_op jit(solution)/shard_map/while/body/eval_jaxpr/ppermute | solution.py:21
  622.2 14.3 %collective-permute-done = f32[6,8,1024]{2,1,0:T(8,128)S(1)} collective-permute-done((f32[6,8,1024]{2,1,0:T(8,128)S(1)}, f32[6,8,1024]{2,1,0:T(8,128)S(1)}, u32[]{:S(2)}, u32[]{:S(2)}) %collective-permute-start) | collective-permute-done | bytes 196640 | tf_op jit(solution)/shard_map/while/body/eval_jaxpr/ppermute | solution.py:21
  639.4 14.3 %collective-permute-done = f32[6,8,1024]{2,1,0:T(8,128)S(1)} collective-permute-done((f32[6,8,1024]{2,1,0:T(8,128)S(1)}, f32[6,8,1024]{2,1,0:T(8,128)S(1)}, u32[]{:S(2)}, u32[]{:S(2)}) %collective-permute-start) | collective-permute-done | bytes 196640 | tf_op jit(solution)/shard_map/while/body/eval_jaxpr/ppermute | solution.py:21
  656.7 14.3 %collective-permute-done = f32[6,8,1024]{2,1,0:T(8,128)S(1)} collective-permute-done((f32[6,8,1024]{2,1,0:T(8,128)S(1)}, f32[6,8,1024]{2,1,0:T(8,128)S(1)}, u32[]{:S(2)}, u32[]{:S(2)}) %collective-permute-start) | collective-permute-done | bytes 196640 | tf_op jit(solution)/shard_map/while/body/eval_jaxpr/ppermute | solution.py:21
  673.9 14.3 %collective-permute-done = f32[6,8,1024]{2,1,0:T(8,128)S(1)} collective-permute-done((f32[6,8,1024]{2,1,0:T(8,128)S(1)}, f32[6,8,1024]{2,1,0:T(8,128)S(1)}, u32[]{:S(2)}, u32[]{:S(2)}) %collective-permute-start) | collective-permute-done | bytes 196640 | tf_op jit(solution)/shard_map/while/body/eval_jaxpr/ppermute | solution.py:21
  691.2 14.3 %collective-permute-done = f32[6,8,1024]{2,1,0:T(8,128)S(1)} collective-permute-done((f32[6,8,1024]{2,1,0:T(8,128)S(1)}, f32[6,8,1024]{2,1,0:T(8,128)S(1)}, u32[]{:S(2)}, u32[]{:S(2)}) %collective-permute-start) | collective-permute-done | bytes 196640 | tf_op jit(solution)/shard_map/while/body/eval_jaxpr/ppermute | solution.py:21
  708.4 14.3 %collective-permute-done = f32[6,8,1024]{2,1,0:T(8,128)S(1)} collective-permute-done((f32[6,8,1024]{2,1,0:T(8,128)S(1)}, f32[6,8,1024]{2,1,0:T(8,128)S(1)}, u32[]{:S(2)}, u32[]{:S(2)}) %collective-permute-start) | collective-permute-done | bytes 196640 | tf_op jit(solution)/shard_map/while/body/eval_jaxpr/ppermute | solution.py:21
  725.7 14.4 %collective-permute-done = f32[6,8,1024]{2,1,0:T(8,128)S(1)} collective-permute-done((f32[6,8,1024]{2,1,0:T(8,128)S(1)}, f32[6,8,1024]{2,1,0:T(8,128)S(1)}, u32[]{:S(2)}, u32[]{:S(2)}) %collective-permute-start) | collective-permute-done | bytes 196640 | tf_op jit(solution)/shard_map/while/body/eval_jaxpr/ppermute | solution.py:21
  743.0 15.5 %collective-permute-done = f32[6,8,1024]{2,1,0:T(8,128)S(1)} collective-permute-done((f32[6,8,1024]{2,1,0:T(8,128)S(1)}, f32[6,8,1024]{2,1,0:T(8,128)S(1)}, u32[]{:S(2)}, u32[]{:S(2)}) %collective-permute-start) | collective-permute-done | bytes 196640 | tf_op jit(solution)/shard_map/while/body/eval_jaxpr/ppermute | solution.py:21
  761.4 14.3 %collective-permute-done = f32[6,8,1024]{2,1,0:T(8,128)S(1)} collective-permute-done((f32[6,8,1024]{2,1,0:T(8,128)S(1)}, f32[6,8,1024]{2,1,0:T(8,128)S(1)}, u32[]{:S(2)}, u32[]{:S(2)}) %collective-permute-start) | collective-permute-done | bytes 196640 | tf_op jit(solution)/shard_map/while/body/eval_jaxpr/ppermute | solution.py:21
  778.7 14.3 %collective-permute-done = f32[6,8,1024]{2,1,0:T(8,128)S(1)} collective-permute-done((f32[6,8,1024]{2,1,0:T(8,128)S(1)}, f32[6,8,1024]{2,1,0:T(8,128)S(1)}, u32[]{:S(2)}, u32[]{:S(2)}) %collective-permute-start) | collective-permute-done | bytes 196640 | tf_op jit(solution)/shard_map/while/body/eval_jaxpr/ppermute | solution.py:21
  (157 shorter events, 143.3 us)
Async XLA Ops:
  0.6 18.4 %copy-start.6 = (bf16[128,512]{1,0:T(8,128)(2,1)S(1)}, bf16[128,512]{1,0:T(8,128)(2,1)}, u32[]{:S(2)}) copy-start(bf16[128,512]{1,0:T(8,128)(2,1)} %param.6) | copy-start | bytes 393220
  0.6 36.8 %copy-start.11 = (s32[6,4]{0,1:T(4,128)S(1)}, s32[6,4]{0,1:T(4,128)}, u32[]{:S(2)}) copy-start(s32[6,4]{0,1:T(4,128)} %param.9) | copy-start | bytes 292
  3.6 167.4 %all-to-all-start = ((bf16[32,6,8,1024]{3,2,1,0:T(8,128)(2,1)}), bf16[32,6,8,1024]{3,2,1,0:T(8,128)(2,1)S(1)}, u32[]{:S(2)}, u32[]{:S(2)}) async-start(bf16[32,6,8,1024]{3,2,1,0:T(8,128)(2,1)} %stack.4), calls=%async_computation | async-start | bytes 6291456 | tf_op jit(solution)/shard_map/all_to_all | solution.py:46
  19.8 158.8 %collective-permute-start.4 = (bf16[128,512]{0,1:T(8,128)(2,1)}, bf16[128,512]{0,1:T(8,128)(2,1)}, u32[]{:S(2)}, u32[]{:S(2)}) collective-permute-start(bf16[128,512]{0,1:T(8,128)(2,1)} %copy.82), channel_id=1, source_target_pairs={{0,8},{8,0},{1,9},{9,1},{2,10},{10,2},{3,11},{11,3},{4,12},{12,4},... | collective-permute-start | bytes 393224 | tf_op jit(solution)/shard_map/ppermute | solution.py:16
  28.0 151.8 %collective-permute-start.3 = (bf16[128,512]{0,1:T(8,128)(2,1)}, bf16[128,512]{0,1:T(8,128)(2,1)}, u32[]{:S(2)}, u32[]{:S(2)}) collective-permute-start(bf16[128,512]{0,1:T(8,128)(2,1)} %copy.82), channel_id=1, source_target_pairs={{0,4},{4,0},{1,5},{5,1},{2,6},{6,2},{3,7},{7,3},{8,12},{12,8},{9,1... | collective-permute-start | bytes 393224 | tf_op jit(solution)/shard_map/ppermute | solution.py:16
  32.2 148.9 %collective-permute-start.2 = (bf16[128,512]{0,1:T(8,128)(2,1)}, bf16[128,512]{0,1:T(8,128)(2,1)}, u32[]{:S(2)}, u32[]{:S(2)}) collective-permute-start(bf16[128,512]{0,1:T(8,128)(2,1)} %copy.82), channel_id=1, source_target_pairs={{0,2},{2,0},{1,3},{3,1},{4,6},{6,4},{5,7},{7,5},{8,10},{10,8},{9,1... | collective-permute-start | bytes 393224 | tf_op jit(solution)/shard_map/ppermute | solution.py:16
  35.5 146.8 %collective-permute-start.1 = (bf16[128,512]{0,1:T(8,128)(2,1)}, bf16[128,512]{0,1:T(8,128)(2,1)}, u32[]{:S(2)}, u32[]{:S(2)}) collective-permute-start(bf16[128,512]{0,1:T(8,128)(2,1)} %copy.82), channel_id=1, source_target_pairs={{0,1},{1,0},{2,3},{3,2},{4,5},{5,4},{6,7},{7,6},{8,9},{9,8},{10,11... | collective-permute-start | bytes 393224 | tf_op jit(solution)/shard_map/ppermute | solution.py:16
  178.5 9.1 %copy-start.5 = (bf16[1,256,1024]{1,2,0:T(8,128)(2,1)S(1)}, bf16[1,256,1024]{1,2,0:T(8,128)(2,1)}, u32[]{:S(2)}) copy-start(bf16[1,256,1024]{1,2,0:T(8,128)(2,1)} %copy.81) | copy-start | bytes 1572868
  179.8 10.2 %copy-start.7 = (bf16[128,1,2,1,256]{4,0,2,3,1:T(8,128)(2,1)S(1)}, bf16[128,1,2,1,256]{4,0,2,3,1:T(8,128)(2,1)}, u32[]{:S(2)}) copy-start(bf16[128,1,2,1,256]{4,0,2,3,1:T(8,128)(2,1)} %rev.4) | copy-start | bytes 393220
  198.0 597.0 %collective-permute-start.8 = (f32[128,512]{0,1:T(8,128)}, f32[128,512]{0,1:T(8,128)S(1)}, u32[]{:S(2)}, u32[]{:S(2)}) collective-permute-start(f32[128,512]{0,1:T(8,128)} %bitcast.28), channel_id=1, source_target_pairs={{0,8},{8,0},{1,9},{9,1},{2,10},{10,2},{3,11},{11,3},{4,12},{12,4},... | collective-permute-start | bytes 786440 | tf_op jit(solution)/shard_map/ppermute | solution.py:16
  206.2 588.8 %collective-permute-start.7 = (f32[128,512]{0,1:T(8,128)}, f32[128,512]{0,1:T(8,128)}, u32[]{:S(2)}, u32[]{:S(2)}) collective-permute-start(f32[128,512]{0,1:T(8,128)} %bitcast.25), channel_id=1, source_target_pairs={{0,4},{4,0},{1,5},{5,1},{2,6},{6,2},{3,7},{7,3},{8,12},{12,8},{9,1... | collective-permute-start | bytes 786440 | tf_op jit(solution)/shard_map/ppermute | solution.py:16
  210.4 584.6 %collective-permute-start.6 = (f32[128,512]{0,1:T(8,128)}, f32[128,512]{0,1:T(8,128)}, u32[]{:S(2)}, u32[]{:S(2)}) collective-permute-start(f32[128,512]{0,1:T(8,128)} %bitcast.22), channel_id=1, source_target_pairs={{0,2},{2,0},{1,3},{3,1},{4,6},{6,4},{5,7},{7,5},{8,10},{10,8},{9,1... | collective-permute-start | bytes 786440 | tf_op jit(solution)/shard_map/ppermute | solution.py:16
  213.7 581.4 %collective-permute-start.5 = (f32[128,512]{0,1:T(8,128)}, f32[128,512]{0,1:T(8,128)}, u32[]{:S(2)}, u32[]{:S(2)}) collective-permute-start(f32[128,512]{0,1:T(8,128)} %bitcast.19), channel_id=1, source_target_pairs={{0,1},{1,0},{2,3},{3,2},{4,5},{5,4},{6,7},{7,6},{8,9},{9,8},{10,11... | collective-permute-start | bytes 786440 | tf_op jit(solution)/shard_map/ppermute | solution.py:16
  238.6 7.7 copy-start
  241.8 6.4 copy-start.10
  243.0 4.9 copy-start.1
  243.0 5.3 copy-start.9
  251.2 17.9 %collective-permute-start = (f32[6,8,1024]{2,1,0:T(8,128)S(1)}, f32[6,8,1024]{2,1,0:T(8,128)S(1)}, u32[]{:S(2)}, u32[]{:S(2)}) collective-permute-start(f32[6,8,1024]{2,1,0:T(8,128)S(1)} %get-tuple-element.223), channel_id=1, source_target_pairs={{0,16},{16,32},{32,48},{48,64},{64,80},{80,96},{96,112},{112,128},... | collective-permute-start | bytes 589832 | tf_op jit(solution)/shard_map/while/body/eval_jaxpr/ppermute | solution.py:21
  270.1 17.1 %collective-permute-start = (f32[6,8,1024]{2,1,0:T(8,128)S(1)}, f32[6,8,1024]{2,1,0:T(8,128)S(1)}, u32[]{:S(2)}, u32[]{:S(2)}) collective-permute-start(f32[6,8,1024]{2,1,0:T(8,128)S(1)} %get-tuple-element.223), channel_id=1, source_target_pairs={{0,16},{16,32},{32,48},{48,64},{64,80},{80,96},{96,112},{112,128},... | collective-permute-start | bytes 589832 | tf_op jit(solution)/shard_map/while/body/eval_jaxpr/ppermute | solution.py:21
  288.1 16.3 %collective-permute-start = (f32[6,8,1024]{2,1,0:T(8,128)S(1)}, f32[6,8,1024]{2,1,0:T(8,128)S(1)}, u32[]{:S(2)}, u32[]{:S(2)}) collective-permute-start(f32[6,8,1024]{2,1,0:T(8,128)S(1)} %get-tuple-element.223), channel_id=1, source_target_pairs={{0,16},{16,32},{32,48},{48,64},{64,80},{80,96},{96,112},{112,128},... | collective-permute-start | bytes 589832 | tf_op jit(solution)/shard_map/while/body/eval_jaxpr/ppermute | solution.py:21
  305.4 16.3 %collective-permute-start = (f32[6,8,1024]{2,1,0:T(8,128)S(1)}, f32[6,8,1024]{2,1,0:T(8,128)S(1)}, u32[]{:S(2)}, u32[]{:S(2)}) collective-permute-start(f32[6,8,1024]{2,1,0:T(8,128)S(1)} %get-tuple-element.223), channel_id=1, source_target_pairs={{0,16},{16,32},{32,48},{48,64},{64,80},{80,96},{96,112},{112,128},... | collective-permute-start | bytes 589832 | tf_op jit(solution)/shard_map/while/body/eval_jaxpr/ppermute | solution.py:21
  322.6 16.3 %collective-permute-start = (f32[6,8,1024]{2,1,0:T(8,128)S(1)}, f32[6,8,1024]{2,1,0:T(8,128)S(1)}, u32[]{:S(2)}, u32[]{:S(2)}) collective-permute-start(f32[6,8,1024]{2,1,0:T(8,128)S(1)} %get-tuple-element.223), channel_id=1, source_target_pairs={{0,16},{16,32},{32,48},{48,64},{64,80},{80,96},{96,112},{112,128},... | collective-permute-start | bytes 589832 | tf_op jit(solution)/shard_map/while/body/eval_jaxpr/ppermute | solution.py:21
  339.8 16.3 %collective-permute-start = (f32[6,8,1024]{2,1,0:T(8,128)S(1)}, f32[6,8,1024]{2,1,0:T(8,128)S(1)}, u32[]{:S(2)}, u32[]{:S(2)}) collective-permute-start(f32[6,8,1024]{2,1,0:T(8,128)S(1)} %get-tuple-element.223), channel_id=1, source_target_pairs={{0,16},{16,32},{32,48},{48,64},{64,80},{80,96},{96,112},{112,128},... | collective-permute-start | bytes 589832 | tf_op jit(solution)/shard_map/while/body/eval_jaxpr/ppermute | solution.py:21
  357.1 16.3 %collective-permute-start = (f32[6,8,1024]{2,1,0:T(8,128)S(1)}, f32[6,8,1024]{2,1,0:T(8,128)S(1)}, u32[]{:S(2)}, u32[]{:S(2)}) collective-permute-start(f32[6,8,1024]{2,1,0:T(8,128)S(1)} %get-tuple-element.223), channel_id=1, source_target_pairs={{0,16},{16,32},{32,48},{48,64},{64,80},{80,96},{96,112},{112,128},... | collective-permute-start | bytes 589832 | tf_op jit(solution)/shard_map/while/body/eval_jaxpr/ppermute | solution.py:21
  374.3 16.3 %collective-permute-start = (f32[6,8,1024]{2,1,0:T(8,128)S(1)}, f32[6,8,1024]{2,1,0:T(8,128)S(1)}, u32[]{:S(2)}, u32[]{:S(2)}) collective-permute-start(f32[6,8,1024]{2,1,0:T(8,128)S(1)} %get-tuple-element.223), channel_id=1, source_target_pairs={{0,16},{16,32},{32,48},{48,64},{64,80},{80,96},{96,112},{112,128},... | collective-permute-start | bytes 589832 | tf_op jit(solution)/shard_map/while/body/eval_jaxpr/ppermute | solution.py:21
  391.6 16.3 %collective-permute-start = (f32[6,8,1024]{2,1,0:T(8,128)S(1)}, f32[6,8,1024]{2,1,0:T(8,128)S(1)}, u32[]{:S(2)}, u32[]{:S(2)}) collective-permute-start(f32[6,8,1024]{2,1,0:T(8,128)S(1)} %get-tuple-element.223), channel_id=1, source_target_pairs={{0,16},{16,32},{32,48},{48,64},{64,80},{80,96},{96,112},{112,128},... | collective-permute-start | bytes 589832 | tf_op jit(solution)/shard_map/while/body/eval_jaxpr/ppermute | solution.py:21
  408.8 16.3 %collective-permute-start = (f32[6,8,1024]{2,1,0:T(8,128)S(1)}, f32[6,8,1024]{2,1,0:T(8,128)S(1)}, u32[]{:S(2)}, u32[]{:S(2)}) collective-permute-start(f32[6,8,1024]{2,1,0:T(8,128)S(1)} %get-tuple-element.223), channel_id=1, source_target_pairs={{0,16},{16,32},{32,48},{48,64},{64,80},{80,96},{96,112},{112,128},... | collective-permute-start | bytes 589832 | tf_op jit(solution)/shard_map/while/body/eval_jaxpr/ppermute | solution.py:21
  426.1 16.3 %collective-permute-start = (f32[6,8,1024]{2,1,0:T(8,128)S(1)}, f32[6,8,1024]{2,1,0:T(8,128)S(1)}, u32[]{:S(2)}, u32[]{:S(2)}) collective-permute-start(f32[6,8,1024]{2,1,0:T(8,128)S(1)} %get-tuple-element.223), channel_id=1, source_target_pairs={{0,16},{16,32},{32,48},{48,64},{64,80},{80,96},{96,112},{112,128},... | collective-permute-start | bytes 589832 | tf_op jit(solution)/shard_map/while/body/eval_jaxpr/ppermute | solution.py:21
  443.3 16.3 %collective-permute-start = (f32[6,8,1024]{2,1,0:T(8,128)S(1)}, f32[6,8,1024]{2,1,0:T(8,128)S(1)}, u32[]{:S(2)}, u32[]{:S(2)}) collective-permute-start(f32[6,8,1024]{2,1,0:T(8,128)S(1)} %get-tuple-element.223), channel_id=1, source_target_pairs={{0,16},{16,32},{32,48},{48,64},{64,80},{80,96},{96,112},{112,128},... | collective-permute-start | bytes 589832 | tf_op jit(solution)/shard_map/while/body/eval_jaxpr/ppermute | solution.py:21
  460.6 16.3 %collective-permute-start = (f32[6,8,1024]{2,1,0:T(8,128)S(1)}, f32[6,8,1024]{2,1,0:T(8,128)S(1)}, u32[]{:S(2)}, u32[]{:S(2)}) collective-permute-start(f32[6,8,1024]{2,1,0:T(8,128)S(1)} %get-tuple-element.223), channel_id=1, source_target_pairs={{0,16},{16,32},{32,48},{48,64},{64,80},{80,96},{96,112},{112,128},... | collective-permute-start | bytes 589832 | tf_op jit(solution)/shard_map/while/body/eval_jaxpr/ppermute | solution.py:21
  477.8 17.1 %collective-permute-start = (f32[6,8,1024]{2,1,0:T(8,128)S(1)}, f32[6,8,1024]{2,1,0:T(8,128)S(1)}, u32[]{:S(2)}, u32[]{:S(2)}) collective-permute-start(f32[6,8,1024]{2,1,0:T(8,128)S(1)} %get-tuple-element.223), channel_id=1, source_target_pairs={{0,16},{16,32},{32,48},{48,64},{64,80},{80,96},{96,112},{112,128},... | collective-permute-start | bytes 589832 | tf_op jit(solution)/shard_map/while/body/eval_jaxpr/ppermute | solution.py:21
  495.9 18.3 %collective-permute-start = (f32[6,8,1024]{2,1,0:T(8,128)S(1)}, f32[6,8,1024]{2,1,0:T(8,128)S(1)}, u32[]{:S(2)}, u32[]{:S(2)}) collective-permute-start(f32[6,8,1024]{2,1,0:T(8,128)S(1)} %get-tuple-element.223), channel_id=1, source_target_pairs={{0,16},{16,32},{32,48},{48,64},{64,80},{80,96},{96,112},{112,128},... | collective-permute-start | bytes 589832 | tf_op jit(solution)/shard_map/while/body/eval_jaxpr/ppermute | solution.py:21
  515.1 17.5 %collective-permute-start = (f32[6,8,1024]{2,1,0:T(8,128)S(1)}, f32[6,8,1024]{2,1,0:T(8,128)S(1)}, u32[]{:S(2)}, u32[]{:S(2)}) collective-permute-start(f32[6,8,1024]{2,1,0:T(8,128)S(1)} %get-tuple-element.223), channel_id=1, source_target_pairs={{0,16},{16,32},{32,48},{48,64},{64,80},{80,96},{96,112},{112,128},... | collective-permute-start | bytes 589832 | tf_op jit(solution)/shard_map/while/body/eval_jaxpr/ppermute | solution.py:21
  533.6 16.7 %collective-permute-start = (f32[6,8,1024]{2,1,0:T(8,128)S(1)}, f32[6,8,1024]{2,1,0:T(8,128)S(1)}, u32[]{:S(2)}, u32[]{:S(2)}) collective-permute-start(f32[6,8,1024]{2,1,0:T(8,128)S(1)} %get-tuple-element.223), channel_id=1, source_target_pairs={{0,16},{16,32},{32,48},{48,64},{64,80},{80,96},{96,112},{112,128},... | collective-permute-start | bytes 589832 | tf_op jit(solution)/shard_map/while/body/eval_jaxpr/ppermute | solution.py:21
  551.3 16.3 %collective-permute-start = (f32[6,8,1024]{2,1,0:T(8,128)S(1)}, f32[6,8,1024]{2,1,0:T(8,128)S(1)}, u32[]{:S(2)}, u32[]{:S(2)}) collective-permute-start(f32[6,8,1024]{2,1,0:T(8,128)S(1)} %get-tuple-element.223), channel_id=1, source_target_pairs={{0,16},{16,32},{32,48},{48,64},{64,80},{80,96},{96,112},{112,128},... | collective-permute-start | bytes 589832 | tf_op jit(solution)/shard_map/while/body/eval_jaxpr/ppermute | solution.py:21
  568.5 16.3 %collective-permute-start = (f32[6,8,1024]{2,1,0:T(8,128)S(1)}, f32[6,8,1024]{2,1,0:T(8,128)S(1)}, u32[]{:S(2)}, u32[]{:S(2)}) collective-permute-start(f32[6,8,1024]{2,1,0:T(8,128)S(1)} %get-tuple-element.223), channel_id=1, source_target_pairs={{0,16},{16,32},{32,48},{48,64},{64,80},{80,96},{96,112},{112,128},... | collective-permute-start | bytes 589832 | tf_op jit(solution)/shard_map/while/body/eval_jaxpr/ppermute | solution.py:21
  585.7 16.3 %collective-permute-start = (f32[6,8,1024]{2,1,0:T(8,128)S(1)}, f32[6,8,1024]{2,1,0:T(8,128)S(1)}, u32[]{:S(2)}, u32[]{:S(2)}) collective-permute-start(f32[6,8,1024]{2,1,0:T(8,128)S(1)} %get-tuple-element.223), channel_id=1, source_target_pairs={{0,16},{16,32},{32,48},{48,64},{64,80},{80,96},{96,112},{112,128},... | collective-permute-start | bytes 589832 | tf_op jit(solution)/shard_map/while/body/eval_jaxpr/ppermute | solution.py:21
  603.0 16.3 %collective-permute-start = (f32[6,8,1024]{2,1,0:T(8,128)S(1)}, f32[6,8,1024]{2,1,0:T(8,128)S(1)}, u32[]{:S(2)}, u32[]{:S(2)}) collective-permute-start(f32[6,8,1024]{2,1,0:T(8,128)S(1)} %get-tuple-element.223), channel_id=1, source_target_pairs={{0,16},{16,32},{32,48},{48,64},{64,80},{80,96},{96,112},{112,128},... | collective-permute-start | bytes 589832 | tf_op jit(solution)/shard_map/while/body/eval_jaxpr/ppermute | solution.py:21
  620.2 16.3 %collective-permute-start = (f32[6,8,1024]{2,1,0:T(8,128)S(1)}, f32[6,8,1024]{2,1,0:T(8,128)S(1)}, u32[]{:S(2)}, u32[]{:S(2)}) collective-permute-start(f32[6,8,1024]{2,1,0:T(8,128)S(1)} %get-tuple-element.223), channel_id=1, source_target_pairs={{0,16},{16,32},{32,48},{48,64},{64,80},{80,96},{96,112},{112,128},... | collective-permute-start | bytes 589832 | tf_op jit(solution)/shard_map/while/body/eval_jaxpr/ppermute | solution.py:21
  637.5 16.3 %collective-permute-start = (f32[6,8,1024]{2,1,0:T(8,128)S(1)}, f32[6,8,1024]{2,1,0:T(8,128)S(1)}, u32[]{:S(2)}, u32[]{:S(2)}) collective-permute-start(f32[6,8,1024]{2,1,0:T(8,128)S(1)} %get-tuple-element.223), channel_id=1, source_target_pairs={{0,16},{16,32},{32,48},{48,64},{64,80},{80,96},{96,112},{112,128},... | collective-permute-start | bytes 589832 | tf_op jit(solution)/shard_map/while/body/eval_jaxpr/ppermute | solution.py:21
  654.7 16.3 %collective-permute-start = (f32[6,8,1024]{2,1,0:T(8,128)S(1)}, f32[6,8,1024]{2,1,0:T(8,128)S(1)}, u32[]{:S(2)}, u32[]{:S(2)}) collective-permute-start(f32[6,8,1024]{2,1,0:T(8,128)S(1)} %get-tuple-element.223), channel_id=1, source_target_pairs={{0,16},{16,32},{32,48},{48,64},{64,80},{80,96},{96,112},{112,128},... | collective-permute-start | bytes 589832 | tf_op jit(solution)/shard_map/while/body/eval_jaxpr/ppermute | solution.py:21
  672.0 16.3 %collective-permute-start = (f32[6,8,1024]{2,1,0:T(8,128)S(1)}, f32[6,8,1024]{2,1,0:T(8,128)S(1)}, u32[]{:S(2)}, u32[]{:S(2)}) collective-permute-start(f32[6,8,1024]{2,1,0:T(8,128)S(1)} %get-tuple-element.223), channel_id=1, source_target_pairs={{0,16},{16,32},{32,48},{48,64},{64,80},{80,96},{96,112},{112,128},... | collective-permute-start | bytes 589832 | tf_op jit(solution)/shard_map/while/body/eval_jaxpr/ppermute | solution.py:21
  689.2 16.3 %collective-permute-start = (f32[6,8,1024]{2,1,0:T(8,128)S(1)}, f32[6,8,1024]{2,1,0:T(8,128)S(1)}, u32[]{:S(2)}, u32[]{:S(2)}) collective-permute-start(f32[6,8,1024]{2,1,0:T(8,128)S(1)} %get-tuple-element.223), channel_id=1, source_target_pairs={{0,16},{16,32},{32,48},{48,64},{64,80},{80,96},{96,112},{112,128},... | collective-permute-start | bytes 589832 | tf_op jit(solution)/shard_map/while/body/eval_jaxpr/ppermute | solution.py:21
  706.5 16.3 %collective-permute-start = (f32[6,8,1024]{2,1,0:T(8,128)S(1)}, f32[6,8,1024]{2,1,0:T(8,128)S(1)}, u32[]{:S(2)}, u32[]{:S(2)}) collective-permute-start(f32[6,8,1024]{2,1,0:T(8,128)S(1)} %get-tuple-element.223), channel_id=1, source_target_pairs={{0,16},{16,32},{32,48},{48,64},{64,80},{80,96},{96,112},{112,128},... | collective-permute-start | bytes 589832 | tf_op jit(solution)/shard_map/while/body/eval_jaxpr/ppermute | solution.py:21
  723.7 16.3 %collective-permute-start = (f32[6,8,1024]{2,1,0:T(8,128)S(1)}, f32[6,8,1024]{2,1,0:T(8,128)S(1)}, u32[]{:S(2)}, u32[]{:S(2)}) collective-permute-start(f32[6,8,1024]{2,1,0:T(8,128)S(1)} %get-tuple-element.223), channel_id=1, source_target_pairs={{0,16},{16,32},{32,48},{48,64},{64,80},{80,96},{96,112},{112,128},... | collective-permute-start | bytes 589832 | tf_op jit(solution)/shard_map/while/body/eval_jaxpr/ppermute | solution.py:21
  741.0 17.5 %collective-permute-start = (f32[6,8,1024]{2,1,0:T(8,128)S(1)}, f32[6,8,1024]{2,1,0:T(8,128)S(1)}, u32[]{:S(2)}, u32[]{:S(2)}) collective-permute-start(f32[6,8,1024]{2,1,0:T(8,128)S(1)} %get-tuple-element.223), channel_id=1, source_target_pairs={{0,16},{16,32},{32,48},{48,64},{64,80},{80,96},{96,112},{112,128},... | collective-permute-start | bytes 589832 | tf_op jit(solution)/shard_map/while/body/eval_jaxpr/ppermute | solution.py:21
  759.5 16.3 %collective-permute-start = (f32[6,8,1024]{2,1,0:T(8,128)S(1)}, f32[6,8,1024]{2,1,0:T(8,128)S(1)}, u32[]{:S(2)}, u32[]{:S(2)}) collective-permute-start(f32[6,8,1024]{2,1,0:T(8,128)S(1)} %get-tuple-element.223), channel_id=1, source_target_pairs={{0,16},{16,32},{32,48},{48,64},{64,80},{80,96},{96,112},{112,128},... | collective-permute-start | bytes 589832 | tf_op jit(solution)/shard_map/while/body/eval_jaxpr/ppermute | solution.py:21
  776.7 16.3 %collective-permute-start = (f32[6,8,1024]{2,1,0:T(8,128)S(1)}, f32[6,8,1024]{2,1,0:T(8,128)S(1)}, u32[]{:S(2)}, u32[]{:S(2)}) collective-permute-start(f32[6,8,1024]{2,1,0:T(8,128)S(1)} %get-tuple-element.223), channel_id=1, source_target_pairs={{0,16},{16,32},{32,48},{48,64},{64,80},{80,96},{96,112},{112,128},... | collective-permute-start | bytes 589832 | tf_op jit(solution)/shard_map/while/body/eval_jaxpr/ppermute | solution.py:21
  (4 other events, 8.6 us)
